TPU v7x, 128 devices: a whole 4x4x4 slice. The times are simulated.
128 devices in a mesh: seq: 16 (over z, x), exp: 8 (over y, core).
Axes of the slice: x: 4, y: 4, z: 4, core: 2. Of those that a mesh axis runs over, the one named last changes fastest.
Arguments:
- residual_in: bfloat16 [8, 4096, 2048], P('exp', 'seq'), may hold values from -6 to 6
- query_matrix: bfloat16 [8, 4096, 2048], P('exp', 'seq'), may hold values from -6 to 6
- key_vectors: bfloat16 [8, 4096, 2048], P('exp', 'seq'), may hold values from -6 to 6
- value_vectors: bfloat16 [8, 4096, 2048], P('exp', 'seq'), may hold values from -6 to 6
- head_gain: float32 [2048], replicated, may hold values from 0.5 to 1.5
- norm_gain: float32 [2048], replicated, may hold values from 0.5 to 1.5
- expert_ids: int32 [8, 4096, 4], P('exp', 'seq'), may hold values from 0 to 7, all different within a row; in each aligned block of 256 rows (0 to 255, 256 to 511, ..., all dimensions but the last counted through in order) at most 192 rows name the same one
- gate_probs: float32 [8, 4096, 4], P('exp', 'seq'), may hold values from 0.25 to 1
- w_gate: bfloat16 [8, 2048, 1408], P('exp'), may hold values from -0.125 to 0.125
- w_up: bfloat16 [8, 2048, 1408], P('exp'), may hold values from -0.125 to 0.125
- w_down: bfloat16 [8, 1408, 2048], P('exp'), may hold values from -0.15625 to 0.15625
Outputs:
- layer_out: bfloat16 [8, 4096, 2048], P('exp', 'seq')
Inputs may be any that keep to these rules, and one draw needn't show every extreme that they name: `expert_ids`: the 4 experts of one position differ; among the 256 positions of one device, no expert is named by more than 192 routes.
All inputs are finite; a program needn't handle non-finite values.
Results may differ from a plain program's by a relative error of at most 0.013.
Values may be sent and summed in bfloat16 or wider, within the bound.
No kernel may reach another device: no remote copies, remote signals or barrier semaphores. Data moves between devices by JAX's collectives and lax.ppermute only.
A program may use at most 128 MiB of HBM per device.

v0:
```python
import jax
import jax.numpy as jnp
from jax import lax
from jax.sharding import PartitionSpec as P

D = 2048
HEADS = 16
HD = 128
TOP = 4
EXPERTS = 8
CHUNKS = 2


def block_prefix(state):
    blocks = lax.axis_size("seq")
    pieces = state.reshape(blocks, -1)
    gathered = lax.all_to_all(pieces, "seq", split_axis=0, concat_axis=0, tiled=True)
    shifted = jnp.concatenate([jnp.zeros_like(gathered[:1]), gathered[:-1]], axis=0)
    prefixes = lax.cumsum(shifted, axis=0).astype(jnp.bfloat16)
    mine = lax.all_to_all(prefixes, "seq", split_axis=0, concat_axis=0, tiled=True)
    return mine.reshape(state.shape)


def on_device(
    residual_in,
    query_matrix,
    key_vectors,
    value_vectors,
    head_gain,
    norm_gain,
    expert_ids,
    gate_probs,
    w_gate,
    w_up,
    w_down,
):
    positions = residual_in.shape[1]
    queries = query_matrix[0].reshape(positions, HEADS, HD)
    key_rows = key_vectors[0].reshape(positions, HEADS, HD)
    value_rows = value_vectors[0].reshape(positions, HEADS, HD)
    state = jnp.einsum("thd,the->hde", key_rows, value_rows, preferred_element_type=jnp.float32)
    prefix = block_prefix(state)
    causal = jnp.tril(jnp.ones((positions, positions), dtype=bool))
    scores = jnp.einsum("thd,uhd->htu", queries, key_rows, preferred_element_type=jnp.float32)
    weights = jnp.where(causal[None], scores, 0.0).astype(jnp.bfloat16)
    inner = jnp.einsum("htu,uhd->thd", weights, value_rows, preferred_element_type=jnp.float32)
    outer_product = jnp.einsum("thd,hde->the", queries, prefix, preferred_element_type=jnp.float32)
    mixed = inner + outer_product
    mean_square = jnp.mean(mixed * mixed, axis=-1, keepdims=True)
    attn = (mixed * lax.rsqrt(mean_square + 1e-06)).reshape(positions, D) * head_gain
    resid_float = (
        (residual_in[0].astype(jnp.float32) + attn).astype(jnp.bfloat16).astype(jnp.float32)
    )
    row_square = jnp.mean(resid_float * resid_float, axis=-1, keepdims=True)
    normed = (resid_float * lax.rsqrt(row_square + 1e-06) * norm_gain).astype(jnp.bfloat16)
    route_ids = expert_ids[0]
    route_gates = gate_probs[0]
    experts = jnp.arange(EXPERTS, dtype=jnp.int32)
    table = jnp.sum(
        jnp.where(route_ids[:, :, None] == experts[None, None, :], route_gates[:, :, None], 0.0),
        axis=1,
    )
    groups = lax.axis_size("exp")
    me = lax.axis_index("exp")
    local_count = w_gate.shape[0]
    high = table.astype(jnp.bfloat16)
    rest = table - high.astype(jnp.float32)
    middle = rest.astype(jnp.bfloat16)
    low = (rest - middle.astype(jnp.float32)).astype(jnp.bfloat16)
    pad = jnp.zeros((positions, 128 - 3 * EXPERTS), jnp.bfloat16)
    payload = jnp.concatenate([normed, high, middle, low, pad], axis=1)
    chunk = positions // CHUNKS
    outs = []
    for c in range(CHUNKS):
        gathered = lax.all_gather(payload[c * chunk : (c + 1) * chunk], "exp", axis=0, tiled=True)
        rows = gathered[:, :D]
        code = gathered[:, D : D + 3 * EXPERTS].astype(jnp.float32)
        code = lax.dynamic_slice_in_dim(
            code.reshape(-1, 3, EXPERTS), me * local_count, local_count, axis=2
        )
        weight = code[:, 0] + code[:, 1] + code[:, 2]
        gate_part = jnp.einsum("nd,edf->enf", rows, w_gate, preferred_element_type=jnp.float32)
        up_part = jnp.einsum("nd,edf->enf", rows, w_up, preferred_element_type=jnp.float32)
        hidden = (jax.nn.silu(gate_part) * up_part).astype(jnp.bfloat16)
        result = jnp.einsum("enf,efd->end", hidden, w_down, preferred_element_type=jnp.float32)
        result = result.astype(jnp.bfloat16).astype(jnp.float32)
        contrib = jnp.sum(result * weight.T[:, :, None], axis=0).astype(jnp.bfloat16)
        outs.append(lax.psum_scatter(contrib, "exp", scatter_dimension=0, tiled=True))
    combined = jnp.concatenate(outs, axis=0)
    return (resid_float + combined.astype(jnp.float32)).astype(jnp.bfloat16)[None]


def solution(mesh):
    in_specs = (
        P("exp", "seq", None),
        P("exp", "seq", None),
        P("exp", "seq", None),
        P("exp", "seq", None),
        P(),
        P(),
        P("exp", "seq", None),
        P("exp", "seq", None),
        P("exp", None, None),
        P("exp", None, None),
        P("exp", None, None),
    )
    out_specs = P("exp", "seq", None)
    return jax.shard_map(
        on_device, mesh=mesh, in_specs=in_specs, out_specs=out_specs, check_vma=False
    )
```

profile of v0, /device:TPU:0, one launch (start us, length us, event | category | flops | bytes accessed | tf_op | source)
XLA Modules:
  0.0 271.2 jit_solution(12462219032883238043)
XLA Ops:
  6.5 1.5 copy.77
  8.0 1.5 copy.79
  9.5 0.5 fusion.62
  10.0 0.0 copy-start.3
  10.0 0.0 copy-start.4
  10.0 24.9 %all_to_all.15 = f32[16,1,16384]{2,1,0:T(1,128)S(1)} all-to-all(f32[16,1,16384]{2,1,0:T(1,128)S(1)} %bitcast.158), channel_id=1, replica_groups=mesh['seq'=16,'exp'=8] {'seq'}, dimensions={0} | all-to-all | bytes 2097152 | tf_op jit(solution)/shard_map/all_to_all | solution.py:17
  34.9 0.7 reduce-window_convert_fusion
  35.6 0.6 broadcast.54
  36.2 4.6 %reduce.1 = bf16[16,16384]{1,0:T(8,128)(2,1)} reduce(bf16[16,1,16384]{2,1,0:T(2,128)(2,1)S(1)} %reduce-window_convert_fusion, bf16[]{:T(256)} %broadcast.54), dimensions={1}, to_apply=%reduce-window_convert_fusion.reduce_sub_computation | reduce | bytes 1048578 | tf_op jit(solution)/shard_map/block_prefix/reduce_window_sum | solution.py:19
  40.8 2.2 reshape.234
  43.1 4.2 %all-to-all-start.1 = ((bf16[16,2,8192]{2,1,0:T(2,128)(2,1)}), bf16[16,2,8192]{2,1,0:T(2,128)(2,1)}, u32[]{:S(2)}, u32[]{:S(2)}) async-start(bf16[16,2,8192]{2,1,0:T(2,128)(2,1)} %reshape.234), calls=%async_computation.1 | async-start | bytes 1048576 | tf_op jit(solution)/shard_map/all_to_all | solution.py:20
  47.3 0.2 all-gather.5.cloned.1.call-start
  47.6 0.0 copy-done.3
  47.6 0.0 copy-done.4
  47.6 1.5 copy.60
  49.1 2.4 copy.78
  51.5 4.0 %fusion.58 = f32[16,256,128]{1,2,0:T(8,128)} fusion(bf16[256,16,128]{0,2,1:T(8,128)(2,1)S(1)} %bitcast.155, pred[256,256]{1,0:T(8,128)(4,1)S(1)} %iota_compare_fusion, bf16[256,16,128]{2,1,0:T(8,128)(2,1)S(1)} %bitcast.157, bf16[256,16,128]{2,1,0:T(8,128)(2,1)} %bitcast.159), kind=kOutput, calls=%fused_computation.53 | convolution fusion | flops 538968064 | bytes 5308416 | tf_op jit(solution)/shard_map/htu,uhd->thd/dot_general | solution.py:46
  55.5 0.0 copy-start
  55.5 2.3 all-to-all-done.1
  57.8 2.2 reshape.235
  60.0 3.9 %reduce = bf16[16,16384]{1,0:T(8,128)(2,1)} reduce(bf16[16,1,16384]{2,1,0:T(2,128)(2,1)S(1)} %reshape.235, bf16[]{:T(256)} %constant.40), dimensions={1}, to_apply=%all_to_all.12.reduce_sub_computation | reduce | bytes 1048578 | tf_op jit(solution)/shard_map/all_to_all | solution.py:20
  64.0 1.1 copy.80
  65.1 0.0 copy-done
  65.1 0.0 copy-start.1
  65.1 2.2 multiply_reduce_fusion
  67.3 0.0 copy-start.2
  67.3 0.2 broadcast_multiply_fusion
  67.6 0.0 copy-done.1
  67.6 0.5 fusion.55
  68.1 0.0 copy-done.2
  68.1 0.3 fusion.59
  68.5 1.1 fusion.72
  69.5 0.0 all-gather.5.cloned.1.call-update
  69.6 0.0 all-gather.3.cloned.1.call-start
  69.6 0.7 all-gather.3.cloned.1.call-update
  70.3 0.3 reduce-scatter.9.cloned.1.call-start
  70.6 35.1 %all-gather.5.cloned.1.call-done = bf16[1024,2176]{0,1:T(8,128)(2,1)} async-done(((bf16[128,2176]{0,1:T(8,128)(2,1)}), bf16[1024,2176]{0,1:T(8,128)(2,1)}) %all-gather.5.cloned.1.call-update) | async-done | bytes 4456464 | tf_op jit(solution)/shard_map/all_gather | solution.py:75
  105.7 0.8 slice_bitcast_fusion
  106.5 38.5 %all-gather.3.cloned.1.call-done = bf16[1024,2176]{0,1:T(8,128)(2,1)} async-done(((bf16[128,2176]{0,1:T(8,128)(2,1)}), bf16[1024,2176]{0,1:T(8,128)(2,1)}) %all-gather.3.cloned.1.call-update) | async-done | bytes 4456464 | tf_op jit(solution)/shard_map/all_gather | solution.py:75
  145.0 0.8 slice_bitcast_fusion.1
  145.8 11.8 %fusion.9 = f32[1024,1408]{1,0:T(8,128)} fusion(bf16[1,2048,1408]{2,1,0:T(8,128)(2,1)} %param.20, bf16[1024,2176]{0,1:T(8,128)(2,1)} %all-gather.5.cloned.1.call-done), kind=kOutput, calls=%fused_computation.16 | convolution fusion | flops 5905580032 | bytes 15728640 | tf_op jit(solution)/shard_map/nd,edf->enf/dot_general | solution.py:83
  157.7 21.5 %multiply_convert_fusion = bf16[1024,2048]{1,0:T(8,128)(2,1)} fusion(f32[1024]{0:T(1024)S(1)} %bitcast.169, bf16[1,1408,2048]{2,1,0:T(8,128)(2,1)} %param.21, f32[1024,1408]{1,0:T(8,128)} %fusion.9, bf16[1,2048,1408]{2,1,0:T(8,128)(2,1)} %param.19, bf16[1024,2176]{0,1:T(8,128)(2,1)} %all-gather.5.cloned.1.call-done), kind=kOutput, calls=%fused_computation.1 | convolution fusion | flops 11828199424 | bytes 25694208 | tf_op jit(solution)/shard_map/enf,efd->end/dot_general | solution.py:85
  179.1 0.0 reduce-scatter.9.cloned.1.call-update
  179.2 0.3 reduce-scatter.7.cloned.1.call-start
  179.5 11.8 %fusion.11 = f32[1024,1408]{1,0:T(8,128)} fusion(bf16[1,2048,1408]{2,1,0:T(8,128)(2,1)} %param.20, bf16[1024,2176]{0,1:T(8,128)(2,1)} %all-gather.3.cloned.1.call-done), kind=kOutput, calls=%fused_computation.18 | convolution fusion | flops 5905580032 | bytes 15728640 | tf_op jit(solution)/shard_map/nd,edf->enf/dot_general | solution.py:83
  191.3 21.8 %multiply_convert_fusion.1 = bf16[1024,2048]{1,0:T(8,128)(2,1)} fusion(f32[1024]{0:T(1024)S(1)} %bitcast.170, bf16[1,1408,2048]{2,1,0:T(8,128)(2,1)} %param.21, f32[1024,1408]{1,0:T(8,128)} %fusion.11, bf16[1,2048,1408]{2,1,0:T(8,128)(2,1)} %param.19, bf16[1024,2176]{0,1:T(8,128)(2,1)} %all-gather.3.cloned.1.call-done), kind=kOutput, calls=%fused_computation.2 | convolution fusion | flops 11828199424 | bytes 25694208 | tf_op jit(solution)/shard_map/enf,efd->end/dot_general | solution.py:85
  213.1 0.0 reduce-scatter.7.cloned.1.call-update
  213.1 5.1 %reduce-scatter.9.cloned.1.call-done = bf16[128,2048]{1,0:T(8,128)(2,1)} async-done(((bf16[1024,2048]{1,0:T(8,128)(2,1)}), bf16[128,2048]{1,0:T(8,128)(2,1)}) %reduce-scatter.9.cloned.1.call-update) | async-done | bytes 524304
  218.2 2.0 copy.76
  220.3 37.1 %reduce-scatter.7.cloned.1.call-done = bf16[128,2048]{1,0:T(8,128)(2,1)} async-done(((bf16[1024,2048]{1,0:T(8,128)(2,1)}), bf16[128,2048]{1,0:T(8,128)(2,1)}) %reduce-scatter.7.cloned.1.call-update) | async-done | bytes 524304
  257.4 2.1 copy.74
  259.4 3.0 %add_convert_fusion = bf16[1,256,2048]{1,2,0:T(8,128)(2,1)} fusion(f32[256,16,128]{0,2,1:T(8,128)S(1)} %broadcast_multiply_fusion, bf16[1,256,2048]{1,2,0:T(8,128)(2,1)S(1)} %copy.60, bf16[1,128,2048]{1,2,0:T(8,128)(2,1)} %bitcast.161, bf16[1,128,2048]{1,2,0:T(8,128)(2,1)} %bitcast.162, f32[2048]{0:T(1024)S(1)} %copy-done.1), kind=kLoop, calls=%fused_computation.51 | loop fusion | flops 5767168 | bytes 5251072 | tf_op jit(solution)/shard_map/convert_element_type | solution.py:90
  262.4 2.3 copy.71
  (11 shorter events, 0.1 us)
Async XLA Ops:
  10.0 37.6 %copy-start.3 = (f32[1,256,4]{1,2,0:T(4,128)S(1)}, f32[1,256,4]{1,2,0:T(4,128)}, u32[]{:S(2)}) copy-start(f32[1,256,4]{1,2,0:T(4,128)} %param.18) | copy-start | bytes 12292
  10.0 37.6 %copy-start.4 = (s32[1,256,4]{1,2,0:T(4,128)S(1)}, s32[1,256,4]{1,2,0:T(4,128)}, u32[]{:S(2)}) copy-start(s32[1,256,4]{1,2,0:T(4,128)} %param.17) | copy-start | bytes 12292
  43.1 14.7 %all-to-all-start.1 = ((bf16[16,2,8192]{2,1,0:T(2,128)(2,1)}), bf16[16,2,8192]{2,1,0:T(2,128)(2,1)}, u32[]{:S(2)}, u32[]{:S(2)}) async-start(bf16[16,2,8192]{2,1,0:T(2,128)(2,1)} %reshape.234), calls=%async_computation.1 | async-start | bytes 1048576 | tf_op jit(solution)/shard_map/all_to_all | solution.py:20
  47.3 58.4 %all-gather.5.cloned.1.call-start = ((), (), s32[]{:S(2)}) async-start(), calls=%async_computation.5 | async-start | bytes 5013504 | tf_op jit(solution)/shard_map/all_gather | solution.py:75
  55.5 9.6 %copy-start = (bf16[32,8,16,128]{3,2,1,0:T(8,128)(2,1)S(1)}, bf16[32,8,16,128]{3,2,1,0:T(8,128)(2,1)}, u32[]{:S(2)}) copy-start(bf16[32,8,16,128]{3,2,1,0:T(8,128)(2,1)} %copy.78) | copy-start | bytes 3145732
  65.1 2.5 copy-start.1
  67.3 0.7 copy-start.2
  69.6 75.4 %all-gather.3.cloned.1.call-start = ((), (), s32[]{:S(2)}) async-start(), calls=%async_computation.4 | async-start | bytes 5013504 | tf_op jit(solution)/shard_map/all_gather | solution.py:75
  70.3 147.9 %reduce-scatter.9.cloned.1.call-start = ((), (), s32[]{:S(2)}) async-start(), calls=%async_computation.7 | async-start | bytes 4718592
  179.2 78.2 %reduce-scatter.7.cloned.1.call-start = ((), (), s32[]{:S(2)}) async-start(), calls=%async_computation.6 | async-start | bytes 4718592
Sparse Core Ops, SparseCore 0:
  69.7 36.0 all-gather.4
  107.4 37.5 all-gather.2
  179.3 38.9 reduce-scatter.8
  220.5 36.8 reduce-scatter.6
where the time goes:
time: 272 us; the launch traced here: 271 us
  waiting for transfers between devices  119 us (44%)
  matrix products  73.5 us (27%)
  blocking collectives  24.9 us (9%)
  local copies, waits for them, and re-layouts  22.1 us (8%)
  other arithmetic  13.4 us (5%)
  between operations  13.4 us (5%)
  starting transfers between devices  5.06 us (2%)
    all_gather x2, waiting for transfers between devices, on_device(): lax.all_gather(payload[c * chunk:(c + 1) * chunk], 'exp', axis=0, tiled=T...  73.6 us
    dot_general x2, matrix products, on_device(): jnp.einsum('enf,efd->end', hidden, w_down, preferred_element_type=jnp.flo...  43.2 us
    unnamed x6, waiting for transfers between devices  43 us
    all_to_all x1, blocking collectives, block_prefix(): lax.all_to_all(pieces, 'seq', split_axis=0, concat_axis=0, tiled=True)  24.9 us
    dot_general x2, matrix products, on_device(): jnp.einsum('nd,edf->enf', rows, w_up, preferred_element_type=jnp.float32)  23.7 us
    unnamed x20, local copies, waits for them, and re-layouts  16.7 us
  transfers between devices with their start and end apart: 5, of which 5 were waited for; matrix products, arithmetic and copies ran while one was open for 16% of the time, Pallas kernels for 0%

commit v1 on v0

--- a/solution.py
+++ b/solution.py
@@ -9,6 +9,22 @@
 TOP = 4
 EXPERTS = 8
 CHUNKS = 2
+
+
+def ring_gather(x, axis, dim):
+    ways, here, step = (lax.axis_size(axis), lax.axis_index(axis), x.shape[dim])
+    lengths = [n * ways if d == dim else n for d, n in enumerate(x.shape)]
+    full = lax.dynamic_update_slice_in_dim(jnp.zeros(lengths, x.dtype), x, here * step, axis=dim)
+    going_up = going_down = x
+    for far in range(1, ways // 2 + 1):
+        going_up = lax.ppermute(going_up, axis, [(d, (d + 1) % ways) for d in range(ways)])
+        full = lax.dynamic_update_slice_in_dim(full, going_up, (here - far) % ways * step, axis=dim)
+        if 2 * far < ways:
+            going_down = lax.ppermute(going_down, axis, [(d, (d - 1) % ways) for d in range(ways)])
+            full = lax.dynamic_update_slice_in_dim(
+                full, going_down, (here + far) % ways * step, axis=dim
+            )
+    return full
 
 
 def block_prefix(state):
@@ -72,7 +88,7 @@
     chunk = positions // CHUNKS
     outs = []
     for c in range(CHUNKS):
-        gathered = lax.all_gather(payload[c * chunk : (c + 1) * chunk], "exp", axis=0, tiled=True)
+        gathered = ring_gather(payload[c * chunk : (c + 1) * chunk], "exp", 0)
         rows = gathered[:, :D]
         code = gathered[:, D : D + 3 * EXPERTS].astype(jnp.float32)
         code = lax.dynamic_slice_in_dim(

time: 272 us -> 269 us (0.989)
  waiting for transfers between devices: 119 us -> 72.8 us
  local copies, waits for them, and re-layouts: 22.1 us -> 65.5 us
  blocking collectives: 24.9 us -> 0 us
  starting transfers between devices: 5.06 us -> 24.9 us
  other arithmetic: 13.4 us -> 16.6 us
    all_gather x2 -> x0, waiting for transfers between devices: 73.6 us -> none  [on_device(): lax.all_gather(payload[c * chunk:(c + 1) * chunk], 'exp', axis=0, tiled=T...]
    unnamed x6 -> x2, waiting for transfers between devices: 43 us -> 0.03 us
    reduce_scatter x0 -> x2, waiting for transfers between devices: none -> 36.9 us  [on_device(): lax.psum_scatter(contrib, 'exp', scatter_dimension=0, tiled=True)]
    all_to_all x1 -> x0, blocking collectives: 24.9 us -> none  [block_prefix(): lax.all_to_all(pieces, 'seq', split_axis=0, concat_axis=0, tiled=True)]
    ppermute x0 -> x14, local copies, waits for them, and re-layouts: none -> 21.2 us  [the longest x8 13 us: ring_gather(): lax.ppermute(going_up, axis, [(d, (d + 1) % ways) for d in range(ways)])]
    all_to_all x0 -> x1, waiting for transfers between devices: none -> 17.7 us  [block_prefix(): lax.all_to_all(pieces, 'seq', split_axis=0, concat_axis=0, tiled=True)]
    dynamic_update_slice x0 -> x16, local copies, waits for them, and re-layouts: none -> 17.6 us  [the longest x8 10.3 us: ring_gather(): lax.dynamic_update_slice_in_dim(full, going_up, (here - far) % ways * ste...]
    ppermute x0 -> x14, waiting for transfers between devices: none -> 12.9 us  [the longest x8 12.9 us: ring_gather(): lax.ppermute(going_up, axis, [(d, (d + 1) % ways) for d in range(ways)])]
  transfers between devices with their start and end apart: 5 -> 18, of which waited for: 5 -> 6; matrix products, arithmetic and copies ran while one was open for 16% -> 32% of each run, Pallas kernels for 0% -> 0%
where the time goes in v1:
time: 269 us; the launch traced here: 267 us
  matrix products  73.4 us (27%)
  waiting for transfers between devices  72.8 us (27%)
  local copies, waits for them, and re-layouts  65.5 us (24%)
  starting transfers between devices  24.9 us (9%)
  other arithmetic  16.6 us (6%)
  between operations  13.9 us (5%)
    dot_general x2, matrix products, on_device(): jnp.einsum('enf,efd->end', hidden, w_down, preferred_element_type=jnp.flo...  42.8 us
    reduce_scatter x2, waiting for transfers between devices, on_device(): lax.psum_scatter(contrib, 'exp', scatter_dimension=0, tiled=True)  36.9 us
    dot_general x2, matrix products, on_device(): jnp.einsum('nd,edf->enf', rows, w_gate, preferred_element_type=jnp.float32)  24.3 us
    all_to_all x1, waiting for transfers between devices, block_prefix(): lax.all_to_all(pieces, 'seq', split_axis=0, concat_axis=0, tiled=True)  17.7 us
    ppermute x8, local copies, waits for them, and re-layouts, ring_gather(): lax.ppermute(going_up, axis, [(d, (d + 1) % ways) for d in range(ways)])  13 us
    ppermute x8, waiting for transfers between devices, ring_gather(): lax.ppermute(going_up, axis, [(d, (d + 1) % ways) for d in range(ways)])  12.9 us
    ppermute x6, starting transfers between devices, ring_gather(): lax.ppermute(going_down, axis, [(d, (d - 1) % ways) for d in range(ways)])  11.5 us
    dynamic_update_slice x8, local copies, waits for them, and re-layouts, ring_gather(): lax.dynamic_update_slice_in_dim(full, going_up, (here - far) % ways * ste...  10.3 us
  transfers between devices with their start and end apart: 18, of which 6 were waited for; matrix products, arithmetic and copies ran while one was open for 32% of the time, Pallas kernels for 0%

profile of v1, /device:TPU:0, one launch (start us, length us, event | category | flops | bytes accessed | tf_op | source)
XLA Modules:
  0.0 267.0 jit_solution(11494167517751052896)
XLA Ops:
  6.5 1.5 copy.106
  8.0 1.5 copy.108
  9.5 1.4 fusion.61
  11.0 8.0 %all-to-all-start = ((f32[16,1,16384]{2,1,0:T(1,128)}), f32[16,1,16384]{2,1,0:T(1,128)}, u32[]{:S(2)}, u32[]{:S(2)}) async-start(f32[16,1,16384]{2,1,0:T(1,128)} %bitcast.1), calls=%async_computation | async-start | bytes 2097152 | tf_op jit(solution)/shard_map/all_to_all | solution.py:33
  19.0 17.7 %all-to-all-done = f32[16,1,16384]{2,1,0:T(1,128)} async-done(((f32[16,1,16384]{2,1,0:T(1,128)}), f32[16,1,16384]{2,1,0:T(1,128)}, u32[]{:S(2)}, u32[]{:S(2)}) %all-to-all-start) | async-done | bytes 1048608 | tf_op jit(solution)/shard_map/all_to_all | solution.py:33
  36.7 1.9 reduce-window_convert_fusion
  39.2 4.6 %reduce.1 = bf16[16,16384]{1,0:T(8,128)(2,1)} reduce(bf16[16,1,16384]{2,1,0:T(2,128)(2,1)S(1)} %reduce-window_convert_fusion, bf16[]{:T(256)} %broadcast.65), dimensions={1}, to_apply=%reduce-window_convert_fusion.reduce_sub_computation | reduce | bytes 1048578 | tf_op jit(solution)/shard_map/block_prefix/reduce_window_sum | solution.py:35
  43.8 2.2 reshape.230
  46.0 4.2 %all-to-all-start.1 = ((bf16[16,2,8192]{2,1,0:T(2,128)(2,1)}), bf16[16,2,8192]{2,1,0:T(2,128)(2,1)}, u32[]{:S(2)}, u32[]{:S(2)}) async-start(bf16[16,2,8192]{2,1,0:T(2,128)(2,1)} %reshape.230), calls=%async_computation.1 | async-start | bytes 1048576 | tf_op jit(solution)/shard_map/all_to_all | solution.py:36
  50.8 1.4 copy.107
  52.3 2.7 %fusion.58 = f32[16,256,128]{1,2,0:T(8,128)} fusion(bf16[256,16,128]{0,2,1:T(8,128)(2,1)S(1)} %bitcast.146, pred[256,256]{1,0:T(8,128)(4,1)S(1)} %iota_compare_fusion, bf16[256,16,128]{2,1,0:T(8,128)(2,1)S(1)} %bitcast.148, bf16[256,16,128]{2,1,0:T(8,128)(2,1)S(1)} %bitcast.149), kind=kOutput, calls=%fused_computation.51 | convolution fusion | flops 538968064 | bytes 5308416 | tf_op jit(solution)/shard_map/htu,uhd->thd/dot_general | solution.py:62
  55.0 5.3 %all-to-all-done.1 = bf16[16,2,8192]{2,1,0:T(2,128)(2,1)} async-done(((bf16[16,2,8192]{2,1,0:T(2,128)(2,1)}), bf16[16,2,8192]{2,1,0:T(2,128)(2,1)}, u32[]{:S(2)}, u32[]{:S(2)}) %all-to-all-start.1) | async-done | bytes 524320 | tf_op jit(solution)/shard_map/all_to_all | solution.py:36
  60.3 2.2 reshape.231
  62.6 3.1 %reduce = bf16[16,16384]{1,0:T(8,128)(2,1)S(1)} reduce(bf16[16,1,16384]{2,1,0:T(2,128)(2,1)S(1)} %reshape.231, bf16[]{:T(256)} %constant.108), dimensions={1}, to_apply=%all_to_all.12.reduce_sub_computation | reduce | bytes 1048578 | tf_op jit(solution)/shard_map/all_to_all | solution.py:36
  65.8 2.2 multiply_reduce_fusion
  68.3 1.8 copy.85
  70.2 2.1 fusion.55
  72.3 1.3 fusion.57
  73.6 2.4 concatenate.18
  75.9 1.1 fusion.71
  77.0 1.4 copy.89
  78.9 1.4 copy.97
  80.2 2.6 collective-permute-start.8
  82.9 2.7 broadcast.63.clone
  85.5 0.9 constant_dynamic-update-slice_fusion.7
  86.5 2.7 %broadcast.63.clone.1 = bf16[1024,2176]{0,1:T(8,128)(2,1)} broadcast(bf16[]{:T(256)} %constant.83.clone.1), dimensions={} | broadcast | bytes 4456450 | tf_op jit(solution)/shard_map/broadcast.3
  89.2 0.9 constant_dynamic-update-slice_fusion.15
  90.1 1.4 copy.91
  91.4 3.0 %collective-permute-start.3 = (bf16[128,2176]{1,0:T(8,128)(2,1)}, bf16[128,2176]{1,0:T(8,128)(2,1)}, u32[]{:S(2)}, u32[]{:S(2)}) collective-permute-start(bf16[128,2176]{1,0:T(8,128)(2,1)} %collective-permute-done.1), channel_id=1, source_target_pairs={{0,7},{1,0},{2,1},{3,2},{4,3},{5,4},{6,5},{7,6},{8,15},{9,8},{10,9... | collective-permute-start | bytes 1671176 | tf_op jit(solution)/shard_map/ppermute | solution.py:23
  94.4 1.4 copy.90
  95.8 2.1 copy.98
  97.9 2.0 constant_dynamic-update-slice_fusion.6
  99.9 0.9 constant_dynamic-update-slice_fusion.14
  100.8 1.4 copy.99
  102.1 2.9 %collective-permute-start.10 = (bf16[128,2176]{1,0:T(8,128)(2,1)}, bf16[128,2176]{1,0:T(8,128)(2,1)}, u32[]{:S(2)}, u32[]{:S(2)}) collective-permute-start(bf16[128,2176]{1,0:T(8,128)(2,1)} %collective-permute-done.8), channel_id=1, source_target_pairs={{0,7},{1,0},{2,1},{3,2},{4,3},{5,4},{6,5},{7,6},{8,15},{9,8},{10,9... | collective-permute-start | bytes 1671176 | tf_op jit(solution)/shard_map/ppermute | solution.py:23
  105.0 0.9 constant_dynamic-update-slice_fusion.5
  105.9 0.9 constant_dynamic-update-slice_fusion.13
  106.8 1.4 copy.93
  108.2 3.0 %collective-permute-start.5 = (bf16[128,2176]{1,0:T(8,128)(2,1)}, bf16[128,2176]{1,0:T(8,128)(2,1)}, u32[]{:S(2)}, u32[]{:S(2)}) collective-permute-start(bf16[128,2176]{1,0:T(8,128)(2,1)} %collective-permute-done.3), channel_id=1, source_target_pairs={{0,7},{1,0},{2,1},{3,2},{4,3},{5,4},{6,5},{7,6},{8,15},{9,8},{10,9... | collective-permute-start | bytes 1671176 | tf_op jit(solution)/shard_map/ppermute | solution.py:23
  111.2 1.4 copy.92
  112.5 3.0 %collective-permute-done.9 = bf16[128,2176]{1,0:T(8,128)(2,1)} collective-permute-done((bf16[128,2176]{1,0:T(8,128)(2,1)}, bf16[128,2176]{1,0:T(8,128)(2,1)}, u32[]{:S(2)}, u32[]{:S(2)}) %collective-permute-start.9) | collective-permute-done | bytes 557088 | tf_op jit(solution)/shard_map/ppermute | solution.py:20
  115.5 2.1 copy.100
  117.6 2.0 constant_dynamic-update-slice_fusion.4
  120.4 1.4 copy.101
  122.3 0.9 constant_dynamic-update-slice_fusion.3
  123.2 0.9 constant_dynamic-update-slice_fusion.11
  124.1 1.4 copy.94
  125.5 6.8 %collective-permute-done.11 = bf16[128,2176]{1,0:T(8,128)(2,1)} collective-permute-done((bf16[128,2176]{1,0:T(8,128)(2,1)}, bf16[128,2176]{1,0:T(8,128)(2,1)}, u32[]{:S(2)}, u32[]{:S(2)}) %collective-permute-start.11) | collective-permute-done | bytes 557088 | tf_op jit(solution)/shard_map/ppermute | solution.py:20
  132.3 2.1 copy.102
  134.4 1.4 copy.95
  135.8 2.0 constant_dynamic-update-slice_fusion.2
  138.6 1.4 copy.103
  140.0 0.9 constant_dynamic-update-slice_fusion.1
  141.7 3.1 %collective-permute-done.13 = bf16[128,2176]{1,0:T(8,128)(2,1)} collective-permute-done((bf16[128,2176]{1,0:T(8,128)(2,1)}, bf16[128,2176]{1,0:T(8,128)(2,1)}, u32[]{:S(2)}, u32[]{:S(2)}) %collective-permute-start.13) | collective-permute-done | bytes 557088 | tf_op jit(solution)/shard_map/ppermute | solution.py:20
  144.9 1.4 copy.104
  146.2 0.9 constant_dynamic-update-slice_fusion
  147.9 1.4 copy.96
  151.0 12.1 %fusion.18 = f32[1024,1408]{1,0:T(8,128)} fusion(bf16[1,2048,1408]{2,1,0:T(8,128)(2,1)} %param.19, bf16[1024,2176]{0,1:T(8,128)(2,1)} %constant_dynamic-update-slice_fusion.8), kind=kOutput, calls=%fused_computation.27 | convolution fusion | flops 5905580032 | bytes 15728640 | tf_op jit(solution)/shard_map/nd,edf->enf/dot_general | solution.py:98
  163.1 21.3 %multiply_convert_fusion.1 = bf16[1024,2048]{1,0:T(8,128)(2,1)} fusion(f32[1024]{0:T(1024)S(1)} %bitcast.159, bf16[1,1408,2048]{2,1,0:T(8,128)(2,1)} %param.21, bf16[1,2048,1408]{2,1,0:T(8,128)(2,1)} %param.20, bf16[1024,2176]{0,1:T(8,128)(2,1)} %constant_dynamic-update-slice_fusion.8, f32[1024,1408]{1,0:T(8,128)} %fusion.18), kind=kOutput, calls=%fused_computation.2 | convolution fusion | flops 11828199424 | bytes 25694208 | tf_op jit(solution)/shard_map/enf,efd->end/dot_general | solution.py:101
  184.5 12.2 %fusion.16 = f32[1024,1408]{1,0:T(8,128)} fusion(bf16[1,2048,1408]{2,1,0:T(8,128)(2,1)} %param.19, bf16[1024,2176]{0,1:T(8,128)(2,1)} %constant_dynamic-update-slice_fusion), kind=kOutput, calls=%fused_computation.25 | convolution fusion | flops 5905580032 | bytes 15728640 | tf_op jit(solution)/shard_map/nd,edf->enf/dot_general | solution.py:98
  196.6 21.5 %multiply_convert_fusion = bf16[1024,2048]{1,0:T(8,128)(2,1)} fusion(f32[1024]{0:T(1024)S(1)} %bitcast.160, bf16[1,1408,2048]{2,1,0:T(8,128)(2,1)} %param.21, bf16[1,2048,1408]{2,1,0:T(8,128)(2,1)} %param.20, bf16[1024,2176]{0,1:T(8,128)(2,1)} %constant_dynamic-update-slice_fusion, f32[1024,1408]{1,0:T(8,128)} %fusion.16), kind=kOutput, calls=%fused_computation.1 | convolution fusion | flops 11828199424 | bytes 25694208 | tf_op jit(solution)/shard_map/enf,efd->end/dot_general | solution.py:101
  218.2 1.8 copy.84
  220.0 36.9 %reduce-scatter.5.cloned.1.call-done = bf16[128,2048]{1,0:T(8,128)(2,1)} async-done(((bf16[1024,2048]{1,0:T(8,128)(2,1)}), bf16[128,2048]{1,0:T(8,128)(2,1)}) %reduce-scatter.5.cloned.1.call-update) | async-done | bytes 524304 | tf_op jit(solution)/shard_map/reduce_scatter | solution.py:104
  256.9 3.3 %add_convert_fusion = bf16[1,256,2048]{2,1,0:T(8,128)(2,1)} fusion(f32[1,256,2048]{2,1,0:T(8,128)} %copy.84, bf16[1,256,2048]{2,1,0:T(8,128)(2,1)S(1)} %copy-done.1, bf16[1,128,2048]{2,1,0:T(8,128)(2,1)} %bitcast.156, bf16[1,128,2048]{2,1,0:T(8,128)(2,1)} %bitcast.155, f32[2048]{0:T(1024)S(1)} %copy-done.2), kind=kLoop, calls=%fused_computation.49 | loop fusion | flops 5767168 | bytes 5251072 | tf_op jit(solution)/shard_map/convert_element_type | solution.py:106
  (59 shorter events, 7.7 us)
Async XLA Ops:
  6.5 12.5 %copy-start.4 = (f32[1,256,4]{1,2,0:T(4,128)S(1)}, f32[1,256,4]{1,2,0:T(4,128)}, u32[]{:S(2)}) copy-start(f32[1,256,4]{1,2,0:T(4,128)} %param.18) | copy-start | bytes 12292
  6.5 12.5 %copy-start.5 = (s32[1,256,4]{1,2,0:T(4,128)S(1)}, s32[1,256,4]{1,2,0:T(4,128)}, u32[]{:S(2)}) copy-start(s32[1,256,4]{1,2,0:T(4,128)} %param.17) | copy-start | bytes 12292
  11.0 25.8 %all-to-all-start = ((f32[16,1,16384]{2,1,0:T(1,128)}), f32[16,1,16384]{2,1,0:T(1,128)}, u32[]{:S(2)}, u32[]{:S(2)}) async-start(f32[16,1,16384]{2,1,0:T(1,128)} %bitcast.1), calls=%async_computation | async-start | bytes 2097152 | tf_op jit(solution)/shard_map/all_to_all | solution.py:33
  46.0 14.3 %all-to-all-start.1 = ((bf16[16,2,8192]{2,1,0:T(2,128)(2,1)}), bf16[16,2,8192]{2,1,0:T(2,128)(2,1)}, u32[]{:S(2)}, u32[]{:S(2)}) async-start(bf16[16,2,8192]{2,1,0:T(2,128)(2,1)} %reshape.230), calls=%async_computation.1 | async-start | bytes 1048576 | tf_op jit(solution)/shard_map/all_to_all | solution.py:36
  50.2 169.8 %reduce-scatter.3.cloned.1.call-start = ((), (), s32[]{:S(2)}) async-start(), calls=%async_computation.4 | async-start | bytes 4718592 | tf_op jit(solution)/shard_map/reduce_scatter | solution.py:104
  68.0 2.2 copy-start
  68.0 2.1 copy-start.2
  68.3 4.0 %copy-start.3 = (f32[2048]{0:T(1024)S(1)}, f32[2048]{0:T(1024)}, u32[]{:S(2)}) copy-start(f32[2048]{0:T(1024)} %param.16) | copy-start | bytes 24580
  78.4 11.7 %collective-permute-start.1 = (bf16[128,2176]{1,0:T(8,128)(2,1)}, bf16[128,2176]{1,0:T(8,128)(2,1)}, u32[]{:S(2)}, u32[]{:S(2)}) collective-permute-start(bf16[128,2176]{1,0:T(8,128)(2,1)} %get-tuple-element.7), channel_id=1, source_target_pairs={{0,7},{1,0},{2,1},{3,2},{4,3},{5,4},{6,5},{7,6},{8,15},{9,8},{10,9... | collective-permute-start | bytes 1671176 | tf_op jit(solution)/shard_map/ppermute | solution.py:23
  78.4 16.0 %collective-permute-start = (bf16[128,2176]{1,0:T(8,128)(2,1)}, bf16[128,2176]{1,0:T(8,128)(2,1)}, u32[]{:S(2)}, u32[]{:S(2)}) collective-permute-start(bf16[128,2176]{1,0:T(8,128)(2,1)} %get-tuple-element.7), channel_id=1, source_target_pairs={{0,1},{1,2},{2,3},{3,4},{4,5},{5,6},{6,7},{7,0},{8,9},{9,10},{10,1... | collective-permute-start | bytes 1671176 | tf_op jit(solution)/shard_map/ppermute | solution.py:20
  80.2 20.5 %collective-permute-start.8 = (bf16[128,2176]{1,0:T(8,128)(2,1)}, bf16[128,2176]{1,0:T(8,128)(2,1)}, u32[]{:S(2)}, u32[]{:S(2)}) collective-permute-start(bf16[128,2176]{1,0:T(8,128)(2,1)} %get-tuple-element.8), channel_id=1, source_target_pairs={{0,7},{1,0},{2,1},{3,2},{4,3},{5,4},{6,5},{7,6},{8,15},{9,8},{10,9... | collective-permute-start | bytes 1671176 | tf_op jit(solution)/shard_map/ppermute | solution.py:23
  82.9 12.9 %collective-permute-start.7 = (bf16[128,2176]{1,0:T(8,128)(2,1)}, bf16[128,2176]{1,0:T(8,128)(2,1)}, u32[]{:S(2)}, u32[]{:S(2)}) collective-permute-start(bf16[128,2176]{1,0:T(8,128)(2,1)} %get-tuple-element.8), channel_id=1, source_target_pairs={{0,1},{1,2},{2,3},{3,4},{4,5},{5,6},{6,7},{7,0},{8,9},{9,10},{10,1... | collective-permute-start | bytes 1671176 | tf_op jit(solution)/shard_map/ppermute | solution.py:20
  91.4 15.4 %collective-permute-start.3 = (bf16[128,2176]{1,0:T(8,128)(2,1)}, bf16[128,2176]{1,0:T(8,128)(2,1)}, u32[]{:S(2)}, u32[]{:S(2)}) collective-permute-start(bf16[128,2176]{1,0:T(8,128)(2,1)} %collective-permute-done.1), channel_id=1, source_target_pairs={{0,7},{1,0},{2,1},{3,2},{4,3},{5,4},{6,5},{7,6},{8,15},{9,8},{10,9... | collective-permute-start | bytes 1671176 | tf_op jit(solution)/shard_map/ppermute | solution.py:23
  95.8 15.4 %collective-permute-start.2 = (bf16[128,2176]{1,0:T(8,128)(2,1)}, bf16[128,2176]{1,0:T(8,128)(2,1)}, u32[]{:S(2)}, u32[]{:S(2)}) collective-permute-start(bf16[128,2176]{1,0:T(8,128)(2,1)} %collective-permute-done), channel_id=1, source_target_pairs={{0,1},{1,2},{2,3},{3,4},{4,5},{5,6},{6,7},{7,0},{8,9},{9,10},{10,1... | collective-permute-start | bytes 1671176 | tf_op jit(solution)/shard_map/ppermute | solution.py:20
  102.1 18.3 %collective-permute-start.10 = (bf16[128,2176]{1,0:T(8,128)(2,1)}, bf16[128,2176]{1,0:T(8,128)(2,1)}, u32[]{:S(2)}, u32[]{:S(2)}) collective-permute-start(bf16[128,2176]{1,0:T(8,128)(2,1)} %collective-permute-done.8), channel_id=1, source_target_pairs={{0,7},{1,0},{2,1},{3,2},{4,3},{5,4},{6,5},{7,6},{8,15},{9,8},{10,9... | collective-permute-start | bytes 1671176 | tf_op jit(solution)/shard_map/ppermute | solution.py:23
  105.0 10.5 %collective-permute-start.9 = (bf16[128,2176]{1,0:T(8,128)(2,1)}, bf16[128,2176]{1,0:T(8,128)(2,1)}, u32[]{:S(2)}, u32[]{:S(2)}) collective-permute-start(bf16[128,2176]{1,0:T(8,128)(2,1)} %collective-permute-done.7), channel_id=1, source_target_pairs={{0,1},{1,2},{2,3},{3,4},{4,5},{5,6},{6,7},{7,0},{8,9},{9,10},{10,1... | collective-permute-start | bytes 1671176 | tf_op jit(solution)/shard_map/ppermute | solution.py:20
  108.2 26.2 %collective-permute-start.5 = (bf16[128,2176]{1,0:T(8,128)(2,1)}, bf16[128,2176]{1,0:T(8,128)(2,1)}, u32[]{:S(2)}, u32[]{:S(2)}) collective-permute-start(bf16[128,2176]{1,0:T(8,128)(2,1)} %collective-permute-done.3), channel_id=1, source_target_pairs={{0,7},{1,0},{2,1},{3,2},{4,3},{5,4},{6,5},{7,6},{8,15},{9,8},{10,9... | collective-permute-start | bytes 1671176 | tf_op jit(solution)/shard_map/ppermute | solution.py:23
  112.5 11.6 %collective-permute-start.4 = (bf16[128,2176]{1,0:T(8,128)(2,1)}, bf16[128,2176]{1,0:T(8,128)(2,1)}, u32[]{:S(2)}, u32[]{:S(2)}) collective-permute-start(bf16[128,2176]{1,0:T(8,128)(2,1)} %collective-permute-done.2), channel_id=1, source_target_pairs={{0,1},{1,2},{2,3},{3,4},{4,5},{5,6},{6,7},{7,0},{8,9},{9,10},{10,1... | collective-permute-start | bytes 1671176 | tf_op jit(solution)/shard_map/ppermute | solution.py:20
  121.8 16.8 %collective-permute-start.12 = (bf16[128,2176]{1,0:T(8,128)(2,1)}, bf16[128,2176]{1,0:T(8,128)(2,1)}, u32[]{:S(2)}, u32[]{:S(2)}) collective-permute-start(bf16[128,2176]{1,0:T(8,128)(2,1)} %collective-permute-done.10), channel_id=1, source_target_pairs={{0,7},{1,0},{2,1},{3,2},{4,3},{5,4},{6,5},{7,6},{8,15},{9,8},{10,9... | collective-permute-start | bytes 1671176 | tf_op jit(solution)/shard_map/ppermute | solution.py:23
  121.8 10.5 %collective-permute-start.11 = (bf16[128,2176]{1,0:T(8,128)(2,1)}, bf16[128,2176]{1,0:T(8,128)(2,1)}, u32[]{:S(2)}, u32[]{:S(2)}) collective-permute-start(bf16[128,2176]{1,0:T(8,128)(2,1)} %collective-permute-done.9), channel_id=1, source_target_pairs={{0,1},{1,2},{2,3},{3,4},{4,5},{5,6},{6,7},{7,0},{8,9},{9,10},{10,1... | collective-permute-start | bytes 1671176 | tf_op jit(solution)/shard_map/ppermute | solution.py:20
  125.5 22.5 %collective-permute-start.6 = (bf16[128,2176]{1,0:T(8,128)(2,1)}, bf16[128,2176]{1,0:T(8,128)(2,1)}, u32[]{:S(2)}, u32[]{:S(2)}) collective-permute-start(bf16[128,2176]{1,0:T(8,128)(2,1)} %collective-permute-done.4), channel_id=1, source_target_pairs={{0,1},{1,2},{2,3},{3,4},{4,5},{5,6},{6,7},{7,0},{8,9},{9,10},{10,1... | collective-permute-start | bytes 1671176 | tf_op jit(solution)/shard_map/ppermute | solution.py:20
  134.4 10.5 %collective-permute-start.13 = (bf16[128,2176]{1,0:T(8,128)(2,1)}, bf16[128,2176]{1,0:T(8,128)(2,1)}, u32[]{:S(2)}, u32[]{:S(2)}) collective-permute-start(bf16[128,2176]{1,0:T(8,128)(2,1)} %collective-permute-done.11), channel_id=1, source_target_pairs={{0,1},{1,2},{2,3},{3,4},{4,5},{5,6},{6,7},{7,0},{8,9},{9,10},{10,1... | collective-permute-start | bytes 1671176 | tf_op jit(solution)/shard_map/ppermute | solution.py:20
  184.4 72.5 %reduce-scatter.5.cloned.1.call-start = ((), (), s32[]{:S(2)}) async-start(), calls=%async_computation.5 | async-start | bytes 4718592 | tf_op jit(solution)/shard_map/reduce_scatter | solution.py:104
  218.2 38.7 %copy-start.1 = (bf16[1,256,2048]{2,1,0:T(8,128)(2,1)S(1)}, bf16[1,256,2048]{2,1,0:T(8,128)(2,1)}, u32[]{:S(2)}) copy-start(bf16[1,256,2048]{2,1,0:T(8,128)(2,1)} %param.11) | copy-start | bytes 3145732
Sparse Core Ops, SparseCore 0:
  184.5 33.0 reduce-scatter.2
  220.0 36.8 reduce-scatter.4
